TPU v7x, 32 devices: a whole 2x2x4 slice. The times are simulated.
32 devices in a mesh: groups: 2 (over x), freq: 16 (over z, y, core).
Axes of the slice: x: 2, y: 2, z: 4, core: 2. Of those that a mesh axis runs over, the one named last changes fastest.
Arguments:
- encoder_input: bfloat16 [64, 2048], P(('groups', 'freq')), parts along dimension 0, may hold values from -6 to 6
- desired_responses: bfloat16 [64, 384, 512], P('groups', 'freq'), parts along dimension 0, may hold values from -6 to 6
- sample_index: int32 [64], P('groups'), parts along dimension 0, may hold values from 0 to 31, each once
- encoder_weight: bfloat16 [2048, 512], replicated, may hold values from -0.125 to 0.125
- decoder_weight: bfloat16 [512, 512], replicated, may hold values from -0.25 to 0.25
- frequency_amplitude: bfloat16 [384, 512], P('freq'), may hold values from -4 to 4
- spectral_filter_weight: float32 [2, 256], replicated, may hold values from -4 to 4
- output_weight: bfloat16 [512, 512], replicated, may hold values from -0.25 to 0.25
Outputs:
- grad_enc: float32 [4096, 512], P('groups'), parts along dimension 0
- grad_dec: float32 [1024, 512], P('groups'), parts along dimension 0
- grad_out: float32 [1024, 512], P('groups'), parts along dimension 0
- grad_filter: float32 [4, 256], P('groups'), parts along dimension 0
There are 2 independent parts, one for each index of `groups`. A program takes and returns all parts, laid end to end along the dimension named above; an argument that names none is the same for every part. Nothing has to cross between parts.
Inputs may be any that keep to these rules, and one draw needn't show every extreme that they name: sample_index names each of the 32 samples once.
All inputs are finite; a program needn't handle non-finite values.
Results may differ from a plain program's by a relative error of at most 0.0065.
Values may be sent and summed in bfloat16 or wider, within the bound.
No kernel may reach another device: no remote copies, remote signals or barrier semaphores. Data moves between devices by JAX's collectives and lax.ppermute only.
A program may use at most 128 MiB of HBM per device.

v0:
```python
import math
import jax
import jax.numpy as jnp
from jax import lax
from jax.sharding import PartitionSpec as P


def rotation_tables(antennas):
    indices = jnp.arange(antennas, dtype=jnp.int32)
    products_mod = indices[:, None] * indices[None, :] % antennas
    angle_table = products_mod.astype(jnp.float32) * (2.0 * math.pi / antennas)
    cosine_table = jnp.cos(angle_table) / math.sqrt(antennas)
    sine_table = jnp.sin(angle_table) / math.sqrt(antennas)
    forward_transform = jnp.concatenate(
        [
            jnp.concatenate([cosine_table, -sine_table], 1),
            jnp.concatenate([sine_table, cosine_table], 1),
        ],
        0,
    )
    inverse_transform = jnp.concatenate(
        [
            jnp.concatenate([cosine_table, sine_table], 1),
            jnp.concatenate([-sine_table, cosine_table], 1),
        ],
        0,
    )
    return (forward_transform.astype(jnp.bfloat16), inverse_transform.astype(jnp.bfloat16))


def decode_rows(
    mixed_in,
    wanted_lines,
    output_weight,
    spectral_filter_weight,
    forward_transform,
    inverse_transform,
    loss_scale,
):
    filter_re = spectral_filter_weight[0]
    filter_im = spectral_filter_weight[1]
    spectrum = jnp.dot(mixed_in, forward_transform, preferred_element_type=jnp.float32)
    half_width = spectrum.shape[1] // 2
    spec_re = spectrum[:, :half_width]
    spec_im = spectrum[:, half_width:]
    filtered = jnp.concatenate(
        [spec_re * filter_re - spec_im * filter_im, spec_re * filter_im + spec_im * filter_re], 1
    ).astype(jnp.bfloat16)
    mixed_back = jnp.dot(filtered, inverse_transform, preferred_element_type=jnp.float32)
    hidden = (mixed_in.astype(jnp.float32) + jax.nn.gelu(mixed_back)).astype(jnp.bfloat16)
    rebuilt = hidden.astype(jnp.float32) + jnp.dot(
        hidden, output_weight, preferred_element_type=jnp.float32
    )
    residual = loss_scale * (rebuilt - wanted_lines.astype(jnp.float32))
    residual_half = residual.astype(jnp.bfloat16)
    grad_out = lax.dot_general(
        hidden, residual_half, (((0,), (0,)), ((), ())), preferred_element_type=jnp.float32
    )
    grad_hidden = residual + lax.dot_general(
        residual_half, output_weight, (((1,), (1,)), ((), ())), preferred_element_type=jnp.float32
    )
    grad_mixed = jax.vjp(jax.nn.gelu, mixed_back)[1](grad_hidden)[0].astype(jnp.bfloat16)
    grad_filtered = lax.dot_general(
        grad_mixed, inverse_transform, (((1,), (1,)), ((), ())), preferred_element_type=jnp.float32
    )
    grad_re = grad_filtered[:, :half_width]
    grad_im = grad_filtered[:, half_width:]
    grad_filter = jnp.stack(
        [
            jnp.sum(grad_re * spec_re + grad_im * spec_im, 0),
            jnp.sum(grad_im * spec_re - grad_re * spec_im, 0),
        ]
    )
    grad_spec = jnp.concatenate(
        [grad_re * filter_re + grad_im * filter_im, grad_im * filter_re - grad_re * filter_im], 1
    ).astype(jnp.bfloat16)
    derivative_entering = grad_hidden + lax.dot_general(
        grad_spec, forward_transform, (((1,), (1,)), ((), ())), preferred_element_type=jnp.float32
    )
    return (derivative_entering, grad_out, grad_filter)


def encoder_grads(inputs_rows, codewords, latent_sums, decoder_weight):
    latent_half = latent_sums.astype(jnp.bfloat16)
    grad_dec = lax.dot_general(
        codewords, latent_half, (((0,), (0,)), ((), ())), preferred_element_type=jnp.float32
    )
    grad_codes = lax.dot_general(
        latent_half, decoder_weight, (((1,), (1,)), ((), ())), preferred_element_type=jnp.float32
    )
    grad_pre = (grad_codes * (1.0 - jnp.square(codewords.astype(jnp.float32)))).astype(jnp.bfloat16)
    grad_enc = lax.dot_general(
        inputs_rows, grad_pre, (((0,), (0,)), ((), ())), preferred_element_type=jnp.float32
    )
    return (grad_enc, grad_dec)


def local(
    encoder_input,
    desired_responses,
    sample_index,
    encoder_weight,
    decoder_weight,
    frequency_amplitude,
    spectral_filter_weight,
    output_weight,
):
    samples = sample_index.shape[0]
    sub_dev = desired_responses.shape[1]
    width = desired_responses.shape[2]
    forward_transform, inverse_transform = rotation_tables(width // 2)
    loss_scale = 1.0 / math.sqrt(samples * sub_dev * lax.axis_size("freq"))
    codes_own = jnp.tanh(
        jnp.dot(encoder_input, encoder_weight, preferred_element_type=jnp.float32)
    ).astype(jnp.bfloat16)
    all_codes = lax.all_gather(codes_own, "freq", axis=0, tiled=True)
    inverse_ids = (
        jnp.zeros((samples,), jnp.int32).at[sample_index].set(jnp.arange(samples, dtype=jnp.int32))
    )
    latent = jnp.dot(all_codes[inverse_ids], decoder_weight, preferred_element_type=jnp.float32)
    gain_row_values = frequency_amplitude.astype(jnp.float32)
    mixed_in = (latent[:, None, :] * gain_row_values[None]).astype(jnp.bfloat16).reshape(-1, width)
    wanted_lines = desired_responses.reshape(-1, width)
    derivative_entering, grad_out, grad_filter = decode_rows(
        mixed_in,
        wanted_lines,
        output_weight,
        spectral_filter_weight,
        forward_transform,
        inverse_transform,
        loss_scale,
    )
    derivative_bottleneck = jnp.einsum(
        "orm,rm->om", derivative_entering.reshape(samples, sub_dev, width), gain_row_values
    )
    enc_order = derivative_bottleneck[sample_index]
    owned_rows = lax.psum_scatter(enc_order, "freq", scatter_dimension=0, tiled=True)
    grad_enc, grad_dec = encoder_grads(encoder_input, codes_own, owned_rows, decoder_weight)
    grad_enc, grad_dec, grad_out, grad_filter = lax.psum(
        (grad_enc, grad_dec, grad_out, grad_filter), "freq"
    )
    return (grad_enc, grad_dec, grad_out, grad_filter)


def solution(mesh):
    return jax.shard_map(
        local,
        mesh=mesh,
        in_specs=(
            P(("groups", "freq"), None),
            P("groups", "freq", None),
            P("groups"),
            P(),
            P(),
            P("freq", None),
            P(),
            P(),
        ),
        out_specs=(P("groups", None), P("groups", None), P("groups", None), P("groups", None)),
        check_vma=False,
    )
```

profile of v0, /device:TPU:0, one launch (start us, length us, event | category | flops | bytes accessed | tf_op | source)
XLA Modules:
  0.0 264.4 jit_solution(11074158935546057527)
XLA Ops:
  7.2 0.0 all-reduce.5.cloned.1.call-start
  7.3 1.0 fusion.30
  8.3 1.1 negate_convert_fusion
  9.4 0.7 compare_select_fusion.1
  10.1 0.7 scatter_custom_fusion
  10.8 0.8 fusion.54
  11.6 1.1 fusion.8
  12.7 23.2 %all-gather = bf16[16,2,512]{2,1,0:T(2,128)(2,1)S(1)} all-gather(bf16[1,2,512]{2,1,0:T(2,128)(2,1)S(1)} %bitcast.34), channel_id=1, replica_groups=mesh['groups'=2,'freq'=16] {'freq'}, dimensions={0}, use_global_device_ids=true | all-gather | bytes 34816 | tf_op jit(solution)/shard_map/all_gather | solution.py:116
  35.9 0.6 gather_fusion
  36.5 0.2 fusion.55
  36.7 0.2 multiply_convert_fusion
  36.9 0.6 fusion.34
  37.4 0.2 subtract_convert_fusion.1
  37.7 1.0 add_convert_fusion
  38.7 0.3 copy-done.10
  39.0 0.6 fusion.7
  39.6 1.6 fusion.21
  41.2 0.6 convolution_add_fusion.1
  41.8 1.2 fusion.17
  43.1 0.4 add_reduce_fusion
  43.5 0.2 copy-done.11
  43.7 0.6 dynamic-slice
  45.0 2.3 convolution_add_fusion
  47.3 0.3 multiply_reduce_fusion
  47.6 0.6 gather_fusion.1
  48.2 59.2 %all-reduce.1 = (bf16[32,512]{1,0:T(8,128)(2,1)S(1)}, f32[2,256]{1,0:T(2,128)}) all-reduce(f32[32,512]{1,0:T(8,128)S(1)} %gather_fusion.1, f32[2,256]{1,0:T(2,128)S(1)} %pad_maximum_fusion.4), channel_id=2, replica_groups=mesh['groups'=2,'freq'=16] {'freq'}, use_global_device_ids=true, to_apply=%region_1.2.clone | all-reduce | flops 16896 | bytes 102400
  107.4 1.3 fusion.53
  108.7 3.0 %convolution_bitcast_fusion = f32[2048,512]{0,1:T(8,128)} fusion(bf16[2,2048]{1,0:T(2,128)(2,1)S(1)} %copy-done.8, bf16[512,512]{1,0:T(8,128)(2,1)S(1)} %copy-done.1, bf16[2,512]{1,0:T(2,128)(2,1)S(1)} %fusion.8, bf16[32,512]{1,0:T(8,128)(2,1)S(1)} %get-tuple-element.14, u32[]{:T(128)S(6)} %multiply.6), kind=kOutput, calls=%fused_computation.3 | convolution fusion | flops 5248000 | bytes 4730884 | tf_op jit(solution)/shard_map/dot_general | solution.py:92
  111.8 137.2 %all-reduce.5.cloned.1.call-done = (f32[2048,512]{0,1:T(8,128)}, f32[512,512]{1,0:T(8,128)}, f32[512,512]{1,0:T(8,128)}) async-done(((f32[2048,512]{0,1:T(8,128)}, f32[512,512]{1,0:T(8,128)}, f32[512,512]{1,0:T(8,128)}), (f32[2048,512]{0,1:T(8,128)}, f32[512,512]{1,0:T(8,128)}, f32[512,512]{1,0:T(8,128)})) %all-reduce.5.cloned.1.call-update) | async-done | bytes 6291472 | tf_op jit(solution)/shard_map/psum | solution.py:139
  248.9 5.3 %copy.13 = f32[2048,512]{1,0:T(8,128)} copy(f32[2048,512]{0,1:T(8,128)} %get-tuple-element.16) | data formatting | bytes 8388608
  254.3 2.4 copy.25
  256.6 1.0 copy.26
  (30 shorter events, 0.2 us)
Async XLA Ops:
  7.2 4.4 %copy-start = (bf16[2048,512]{1,0:T(8,128)(2,1)S(1)}, bf16[2048,512]{1,0:T(8,128)(2,1)}, u32[]{:S(2)}) copy-start(bf16[2048,512]{1,0:T(8,128)(2,1)} %param.11) | copy-start | bytes 6291460
  7.2 28.7 %copy-start.9 = (bf16[24,512]{1,0:T(8,128)(2,1)S(1)}, bf16[24,512]{1,0:T(8,128)(2,1)}, u32[]{:S(2)}) copy-start(bf16[24,512]{1,0:T(8,128)(2,1)} %param.13) | copy-start | bytes 73732
  7.2 29.3 %copy-start.1 = (bf16[512,512]{1,0:T(8,128)(2,1)S(1)}, bf16[512,512]{1,0:T(8,128)(2,1)}, u32[]{:S(2)}) copy-start(bf16[512,512]{1,0:T(8,128)(2,1)} %param.12) | copy-start | bytes 1572868
  7.2 241.7 %all-reduce.5.cloned.1.call-start = ((), (), s32[]{:S(2)}) async-start(), calls=%async_computation | async-start | bytes 12582912 | tf_op jit(solution)/shard_map/psum | solution.py:139
  8.3 33.6 %copy-start.5 = (bf16[256,256]{1,0:T(8,128)(2,1)}, bf16[256,256]{1,0:T(8,128)(2,1)S(1)}, u32[]{:S(2)}) copy-start(bf16[256,256]{1,0:T(8,128)(2,1)S(1)} %fusion.30) | copy-start | bytes 393220
  9.4 32.4 %copy-start.6 = (bf16[256,256]{1,0:T(8,128)(2,1)}, bf16[256,256]{1,0:T(8,128)(2,1)S(1)}, u32[]{:S(2)}) copy-start(bf16[256,256]{1,0:T(8,128)(2,1)S(1)} %get-tuple-element.31) | copy-start | bytes 393220
  9.4 32.4 %copy-start.7 = (bf16[256,256]{1,0:T(8,128)(2,1)}, bf16[256,256]{1,0:T(8,128)(2,1)S(1)}, u32[]{:S(2)}) copy-start(bf16[256,256]{1,0:T(8,128)(2,1)S(1)} %get-tuple-element.32) | copy-start | bytes 393220
  37.7 1.0 copy-start.4
  37.7 1.3 copy-start.10
  41.8 1.3 copy-start.2
  43.1 0.7 copy-start.11
  47.2 61.5 %copy-start.8 = (bf16[2,2048]{1,0:T(2,128)(2,1)S(1)}, bf16[2,2048]{1,0:T(2,128)(2,1)}, u32[]{:S(2)}) copy-start(bf16[2,2048]{1,0:T(2,128)(2,1)} %param.8) | copy-start | bytes 24580
  254.3 2.4 copy-start.3
Sparse Core Ops, SparseCore 0:
  111.9 136.9 all-reduce.4
where the time goes:
time: 265 us; the launch traced here: 264 us
  waiting for transfers between devices  137 us (52%)
  blocking collectives  82.4 us (31%)
  between operations  14.9 us (6%)
  matrix products  13.4 us (5%)
  local copies, waits for them, and re-layouts  12.5 us (5%)
  other arithmetic  3.97 us (1%)
    psum x1, waiting for transfers between devices, local(): lax.psum((grad_enc, grad_dec, grad_out, grad_filter), 'freq')  137 us
    unnamed x1, blocking collectives  59.2 us
    all_gather x1, blocking collectives, local(): all_codes = lax.all_gather(codes_own, 'freq', axis=0, tiled=True)  23.2 us
    unnamed x29, local copies, waits for them, and re-layouts  9.8 us
  transfers between devices with their start and end apart: 1, of which 1 were waited for; matrix products, arithmetic and copies ran while one was open for 0% of the time, Pallas kernels for 0%

commit v1 on v0

--- a/solution.py
+++ b/solution.py
@@ -113,7 +113,12 @@
     codes_own = jnp.tanh(
         jnp.dot(encoder_input, encoder_weight, preferred_element_type=jnp.float32)
     ).astype(jnp.bfloat16)
-    all_codes = lax.all_gather(codes_own, "freq", axis=0, tiled=True)
+    ring = [codes_own]
+    for hop in range(15):
+        ring.append(lax.ppermute(ring[-1], "freq", [(dev, (dev + 1) % 16) for dev in range(16)]))
+    all_codes = jnp.roll(
+        jnp.concatenate(ring[::-1], axis=0), (lax.axis_index("freq") + 1) * ring[0].shape[0], axis=0
+    )
     inverse_ids = (
         jnp.zeros((samples,), jnp.int32).at[sample_index].set(jnp.arange(samples, dtype=jnp.int32))
     )

time: 265 us -> 322 us (1.22)
  waiting for transfers between devices: 137 us -> 220 us
  blocking collectives: 82.4 us -> 58.9 us
    ppermute x0 -> x15, waiting for transfers between devices: none -> 82 us  [local(): lax.ppermute(ring[-1], 'freq', [(dev, (dev + 1) % 16) for dev in range(16)])]
    all_gather x1 -> x0, blocking collectives: 23.2 us -> none  [local(): all_codes = lax.all_gather(codes_own, 'freq', axis=0, tiled=True)]
    unnamed x29 -> x26, local copies, waits for them, and re-layouts: 9.8 us -> 10.4 us
  transfers between devices with their start and end apart: 1 -> 16, of which waited for: 1 -> 16; matrix products, arithmetic and copies ran while one was open for 0% -> 1% of each run, Pallas kernels for 0% -> 0%
where the time goes in v1:
time: 322 us
  waiting for transfers between devices  220 us (68%)
  blocking collectives  58.9 us (18%)
  between operations  14.9 us (5%)
  local copies, waits for them, and re-layouts  12.6 us (4%)
  matrix products  11.8 us (4%)
  other arithmetic  3.26 us (1%)
    psum x1, waiting for transfers between devices, local(): lax.psum((grad_enc, grad_dec, grad_out, grad_filter), 'freq')  138 us
    ppermute x15, waiting for transfers between devices, local(): lax.ppermute(ring[-1], 'freq', [(dev, (dev + 1) % 16) for dev in range(16)])  82 us
    unnamed x1, blocking collectives  58.9 us
    unnamed x26, local copies, waits for them, and re-layouts  10.4 us
  transfers between devices with their start and end apart: 16, of which 16 were waited for; matrix products, arithmetic and copies ran while one was open for 1% of the time, Pallas kernels for 0%

profile of v1, /device:TPU:0, one launch (start us, length us, event | category | flops | bytes accessed | tf_op | source)
XLA Modules:
  0.0 321.7 jit_solution(14742233222984866315)
XLA Ops:
  7.3 1.5 copy-done
  8.8 1.1 fusion.8
  10.3 6.3 %collective-permute-done = bf16[2,512]{1,0:T(2,128)(2,1)S(1)} collective-permute-done((bf16[2,512]{1,0:T(2,128)(2,1)S(1)}, bf16[2,512]{1,0:T(2,128)(2,1)S(1)}, u32[]{:S(2)}, u32[]{:S(2)}) %collective-permute-start) | collective-permute-done | bytes 2080 | tf_op jit(solution)/shard_map/ppermute | solution.py:118
  16.6 5.7 %collective-permute-done.1 = bf16[2,512]{1,0:T(2,128)(2,1)S(1)} collective-permute-done((bf16[2,512]{1,0:T(2,128)(2,1)S(1)}, bf16[2,512]{1,0:T(2,128)(2,1)S(1)}, u32[]{:S(2)}, u32[]{:S(2)}) %collective-permute-start.1) | collective-permute-done | bytes 2080 | tf_op jit(solution)/shard_map/ppermute | solution.py:118
  22.3 5.7 %collective-permute-done.2 = bf16[2,512]{1,0:T(2,128)(2,1)S(1)} collective-permute-done((bf16[2,512]{1,0:T(2,128)(2,1)S(1)}, bf16[2,512]{1,0:T(2,128)(2,1)S(1)}, u32[]{:S(2)}, u32[]{:S(2)}) %collective-permute-start.2) | collective-permute-done | bytes 2080 | tf_op jit(solution)/shard_map/ppermute | solution.py:118
  28.0 5.7 %collective-permute-done.3 = bf16[2,512]{1,0:T(2,128)(2,1)S(1)} collective-permute-done((bf16[2,512]{1,0:T(2,128)(2,1)S(1)}, bf16[2,512]{1,0:T(2,128)(2,1)S(1)}, u32[]{:S(2)}, u32[]{:S(2)}) %collective-permute-start.3) | collective-permute-done | bytes 2080 | tf_op jit(solution)/shard_map/ppermute | solution.py:118
  33.7 5.7 %collective-permute-done.4 = bf16[2,512]{1,0:T(2,128)(2,1)S(1)} collective-permute-done((bf16[2,512]{1,0:T(2,128)(2,1)S(1)}, bf16[2,512]{1,0:T(2,128)(2,1)S(1)}, u32[]{:S(2)}, u32[]{:S(2)}) %collective-permute-start.4) | collective-permute-done | bytes 2080 | tf_op jit(solution)/shard_map/ppermute | solution.py:118
  39.4 5.7 %collective-permute-done.5 = bf16[2,512]{1,0:T(2,128)(2,1)S(1)} collective-permute-done((bf16[2,512]{1,0:T(2,128)(2,1)S(1)}, bf16[2,512]{1,0:T(2,128)(2,1)S(1)}, u32[]{:S(2)}, u32[]{:S(2)}) %collective-permute-start.5) | collective-permute-done | bytes 2080 | tf_op jit(solution)/shard_map/ppermute | solution.py:118
  45.1 5.7 %collective-permute-done.6 = bf16[2,512]{1,0:T(2,128)(2,1)S(1)} collective-permute-done((bf16[2,512]{1,0:T(2,128)(2,1)S(1)}, bf16[2,512]{1,0:T(2,128)(2,1)S(1)}, u32[]{:S(2)}, u32[]{:S(2)}) %collective-permute-start.6) | collective-permute-done | bytes 2080 | tf_op jit(solution)/shard_map/ppermute | solution.py:118
  50.9 5.7 %collective-permute-done.7 = bf16[2,512]{1,0:T(2,128)(2,1)S(1)} collective-permute-done((bf16[2,512]{1,0:T(2,128)(2,1)S(1)}, bf16[2,512]{1,0:T(2,128)(2,1)S(1)}, u32[]{:S(2)}, u32[]{:S(2)}) %collective-permute-start.7) | collective-permute-done | bytes 2080 | tf_op jit(solution)/shard_map/ppermute | solution.py:118
  56.6 5.7 %collective-permute-done.8 = bf16[2,512]{1,0:T(2,128)(2,1)S(1)} collective-permute-done((bf16[2,512]{1,0:T(2,128)(2,1)S(1)}, bf16[2,512]{1,0:T(2,128)(2,1)S(1)}, u32[]{:S(2)}, u32[]{:S(2)}) %collective-permute-start.8) | collective-permute-done | bytes 2080 | tf_op jit(solution)/shard_map/ppermute | solution.py:118
  62.3 0.7 scatter_custom_fusion
  63.0 5.0 %collective-permute-done.9 = bf16[2,512]{1,0:T(2,128)(2,1)S(1)} collective-permute-done((bf16[2,512]{1,0:T(2,128)(2,1)S(1)}, bf16[2,512]{1,0:T(2,128)(2,1)S(1)}, u32[]{:S(2)}, u32[]{:S(2)}) %collective-permute-start.9) | collective-permute-done | bytes 2080 | tf_op jit(solution)/shard_map/ppermute | solution.py:118
  68.0 5.7 %collective-permute-done.10 = bf16[2,512]{1,0:T(2,128)(2,1)S(1)} collective-permute-done((bf16[2,512]{1,0:T(2,128)(2,1)S(1)}, bf16[2,512]{1,0:T(2,128)(2,1)S(1)}, u32[]{:S(2)}, u32[]{:S(2)}) %collective-permute-start.10) | collective-permute-done | bytes 2080 | tf_op jit(solution)/shard_map/ppermute | solution.py:118
  73.7 1.1 negate_convert_fusion
  74.8 4.6 %collective-permute-done.11 = bf16[2,512]{1,0:T(2,128)(2,1)S(1)} collective-permute-done((bf16[2,512]{1,0:T(2,128)(2,1)S(1)}, bf16[2,512]{1,0:T(2,128)(2,1)S(1)}, u32[]{:S(2)}, u32[]{:S(2)}) %collective-permute-start.11) | collective-permute-done | bytes 2080 | tf_op jit(solution)/shard_map/ppermute | solution.py:118
  79.4 1.0 fusion.30
  80.4 4.7 %collective-permute-done.12 = bf16[2,512]{1,0:T(2,128)(2,1)S(1)} collective-permute-done((bf16[2,512]{1,0:T(2,128)(2,1)S(1)}, bf16[2,512]{1,0:T(2,128)(2,1)S(1)}, u32[]{:S(2)}, u32[]{:S(2)}) %collective-permute-start.12) | collective-permute-done | bytes 2080 | tf_op jit(solution)/shard_map/ppermute | solution.py:118
  85.1 5.7 %collective-permute-done.13 = bf16[2,512]{1,0:T(2,128)(2,1)S(1)} collective-permute-done((bf16[2,512]{1,0:T(2,128)(2,1)S(1)}, bf16[2,512]{1,0:T(2,128)(2,1)S(1)}, u32[]{:S(2)}, u32[]{:S(2)}) %collective-permute-start.13) | collective-permute-done | bytes 2080 | tf_op jit(solution)/shard_map/ppermute | solution.py:118
  92.1 4.4 %collective-permute-done.14 = bf16[2,512]{1,0:T(2,128)(2,1)S(1)} collective-permute-done((bf16[2,512]{1,0:T(2,128)(2,1)S(1)}, bf16[2,512]{1,0:T(2,128)(2,1)S(1)}, u32[]{:S(2)}, u32[]{:S(2)}) %collective-permute-start.14) | collective-permute-done | bytes 2080 | tf_op jit(solution)/shard_map/ppermute | solution.py:118
  96.8 0.6 gather_fusion
  98.6 1.0 add_convert_fusion
  99.9 0.6 fusion.7
  100.5 1.6 fusion.21
  102.7 1.2 fusion.17
  105.9 58.9 %all-reduce.1 = (bf16[32,512]{1,0:T(8,128)(2,1)S(1)}, f32[2,256]{1,0:T(2,128)}) all-reduce(f32[32,512]{1,0:T(8,128)S(1)} %gather_fusion.1, f32[2,256]{1,0:T(2,128)S(1)} %pad_maximum_fusion.4), channel_id=2, replica_groups=mesh['groups'=2,'freq'=16] {'freq'}, use_global_device_ids=true, to_apply=%region_1.2.clone | all-reduce | flops 16896 | bytes 102400
  164.9 1.3 fusion.53
  166.2 3.0 convolution_bitcast_fusion
  169.2 137.6 %all-reduce.5.cloned.1.call-done = (f32[2048,512]{0,1:T(8,128)}, f32[512,512]{1,0:T(8,128)}, f32[512,512]{1,0:T(8,128)}) async-done(((f32[2048,512]{0,1:T(8,128)}, f32[512,512]{1,0:T(8,128)}, f32[512,512]{1,0:T(8,128)}), (f32[2048,512]{0,1:T(8,128)}, f32[512,512]{1,0:T(8,128)}, f32[512,512]{1,0:T(8,128)})) %all-reduce.5.cloned.1.call-update) | async-done | bytes 6291472 | tf_op jit(solution)/shard_map/psum | solution.py:144
  306.8 5.4 %copy.13 = f32[2048,512]{1,0:T(8,128)} copy(f32[2048,512]{0,1:T(8,128)} %get-tuple-element.16) | data formatting | bytes 8388608
  312.3 1.0 copy.25
  313.9 1.0 copy.26
  (58 shorter events, 6.1 us)
Async XLA Ops:
  7.2 1.6 copy-start
  7.2 83.6 %copy-start.10 = (u32[32]{0:T(128)S(1)}, u32[32]{0:T(128)}, u32[]{:S(2)}) copy-start(u32[32]{0:T(128)} %constant.75) | copy-start | bytes 388
  7.2 43.7 %copy-start.6 = (bf16[24,512]{1,0:T(8,128)(2,1)S(1)}, bf16[24,512]{1,0:T(8,128)(2,1)}, u32[]{:S(2)}) copy-start(bf16[24,512]{1,0:T(8,128)(2,1)} %param.13) | copy-start | bytes 73732
  7.2 49.3 %copy-start.7 = (f32[2,256]{1,0:T(2,128)S(1)}, f32[2,256]{1,0:T(2,128)}, u32[]{:S(2)}) copy-start(f32[2,256]{1,0:T(2,128)} %param.14) | copy-start | bytes 6148
  7.2 55.0 %copy-start.9 = (s32[32]{0:T(128)S(1)}, s32[32]{0:T(128)}, u32[]{:S(2)}) copy-start(s32[32]{0:T(128)} %param.10) | copy-start | bytes 388
  7.2 90.2 %copy-start.1 = (bf16[512,512]{1,0:T(8,128)(2,1)S(1)}, bf16[512,512]{1,0:T(8,128)(2,1)}, u32[]{:S(2)}) copy-start(bf16[512,512]{1,0:T(8,128)(2,1)} %param.12) | copy-start | bytes 1572868
  7.2 299.6 %all-reduce.5.cloned.1.call-start = ((), (), s32[]{:S(2)}) async-start(), calls=%async_computation | async-start | bytes 12582912 | tf_op jit(solution)/shard_map/psum | solution.py:144
  9.9 6.7 %collective-permute-start = (bf16[2,512]{1,0:T(2,128)(2,1)S(1)}, bf16[2,512]{1,0:T(2,128)(2,1)S(1)}, u32[]{:S(2)}, u32[]{:S(2)}) collective-permute-start(bf16[2,512]{1,0:T(2,128)(2,1)S(1)} %fusion.8), channel_id=1, source_target_pairs={{0,1},{1,2},{2,3},{3,4},{4,5},{5,6},{6,7},{7,8},{8,9},{9,10},{10,1... | collective-permute-start | bytes 6152 | tf_op jit(solution)/shard_map/ppermute | solution.py:118
  16.6 5.7 %collective-permute-start.1 = (bf16[2,512]{1,0:T(2,128)(2,1)S(1)}, bf16[2,512]{1,0:T(2,128)(2,1)S(1)}, u32[]{:S(2)}, u32[]{:S(2)}) collective-permute-start(bf16[2,512]{1,0:T(2,128)(2,1)S(1)} %collective-permute-done), channel_id=1, source_target_pairs={{0,1},{1,2},{2,3},{3,4},{4,5},{5,6},{6,7},{7,8},{8,9},{9,10},{10,1... | collective-permute-start | bytes 6152 | tf_op jit(solution)/shard_map/ppermute | solution.py:118
  22.3 5.7 %collective-permute-start.2 = (bf16[2,512]{1,0:T(2,128)(2,1)S(1)}, bf16[2,512]{1,0:T(2,128)(2,1)S(1)}, u32[]{:S(2)}, u32[]{:S(2)}) collective-permute-start(bf16[2,512]{1,0:T(2,128)(2,1)S(1)} %collective-permute-done.1), channel_id=1, source_target_pairs={{0,1},{1,2},{2,3},{3,4},{4,5},{5,6},{6,7},{7,8},{8,9},{9,10},{10,1... | collective-permute-start | bytes 6152 | tf_op jit(solution)/shard_map/ppermute | solution.py:118
  28.0 5.7 %collective-permute-start.3 = (bf16[2,512]{1,0:T(2,128)(2,1)S(1)}, bf16[2,512]{1,0:T(2,128)(2,1)S(1)}, u32[]{:S(2)}, u32[]{:S(2)}) collective-permute-start(bf16[2,512]{1,0:T(2,128)(2,1)S(1)} %collective-permute-done.2), channel_id=1, source_target_pairs={{0,1},{1,2},{2,3},{3,4},{4,5},{5,6},{6,7},{7,8},{8,9},{9,10},{10,1... | collective-permute-start | bytes 6152 | tf_op jit(solution)/shard_map/ppermute | solution.py:118
  33.7 5.7 %collective-permute-start.4 = (bf16[2,512]{1,0:T(2,128)(2,1)S(1)}, bf16[2,512]{1,0:T(2,128)(2,1)S(1)}, u32[]{:S(2)}, u32[]{:S(2)}) collective-permute-start(bf16[2,512]{1,0:T(2,128)(2,1)S(1)} %collective-permute-done.3), channel_id=1, source_target_pairs={{0,1},{1,2},{2,3},{3,4},{4,5},{5,6},{6,7},{7,8},{8,9},{9,10},{10,1... | collective-permute-start | bytes 6152 | tf_op jit(solution)/shard_map/ppermute | solution.py:118
  39.4 5.7 %collective-permute-start.5 = (bf16[2,512]{1,0:T(2,128)(2,1)S(1)}, bf16[2,512]{1,0:T(2,128)(2,1)S(1)}, u32[]{:S(2)}, u32[]{:S(2)}) collective-permute-start(bf16[2,512]{1,0:T(2,128)(2,1)S(1)} %collective-permute-done.4), channel_id=1, source_target_pairs={{0,1},{1,2},{2,3},{3,4},{4,5},{5,6},{6,7},{7,8},{8,9},{9,10},{10,1... | collective-permute-start | bytes 6152 | tf_op jit(solution)/shard_map/ppermute | solution.py:118
  45.1 5.7 %collective-permute-start.6 = (bf16[2,512]{1,0:T(2,128)(2,1)S(1)}, bf16[2,512]{1,0:T(2,128)(2,1)S(1)}, u32[]{:S(2)}, u32[]{:S(2)}) collective-permute-start(bf16[2,512]{1,0:T(2,128)(2,1)S(1)} %collective-permute-done.5), channel_id=1, source_target_pairs={{0,1},{1,2},{2,3},{3,4},{4,5},{5,6},{6,7},{7,8},{8,9},{9,10},{10,1... | collective-permute-start | bytes 6152 | tf_op jit(solution)/shard_map/ppermute | solution.py:118
  50.8 5.7 %collective-permute-start.7 = (bf16[2,512]{1,0:T(2,128)(2,1)S(1)}, bf16[2,512]{1,0:T(2,128)(2,1)S(1)}, u32[]{:S(2)}, u32[]{:S(2)}) collective-permute-start(bf16[2,512]{1,0:T(2,128)(2,1)S(1)} %collective-permute-done.6), channel_id=1, source_target_pairs={{0,1},{1,2},{2,3},{3,4},{4,5},{5,6},{6,7},{7,8},{8,9},{9,10},{10,1... | collective-permute-start | bytes 6152 | tf_op jit(solution)/shard_map/ppermute | solution.py:118
  56.5 5.7 %collective-permute-start.8 = (bf16[2,512]{1,0:T(2,128)(2,1)S(1)}, bf16[2,512]{1,0:T(2,128)(2,1)S(1)}, u32[]{:S(2)}, u32[]{:S(2)}) collective-permute-start(bf16[2,512]{1,0:T(2,128)(2,1)S(1)} %collective-permute-done.7), channel_id=1, source_target_pairs={{0,1},{1,2},{2,3},{3,4},{4,5},{5,6},{6,7},{7,8},{8,9},{9,10},{10,1... | collective-permute-start | bytes 6152 | tf_op jit(solution)/shard_map/ppermute | solution.py:118
  62.3 5.7 %collective-permute-start.9 = (bf16[2,512]{1,0:T(2,128)(2,1)S(1)}, bf16[2,512]{1,0:T(2,128)(2,1)S(1)}, u32[]{:S(2)}, u32[]{:S(2)}) collective-permute-start(bf16[2,512]{1,0:T(2,128)(2,1)S(1)} %collective-permute-done.8), channel_id=1, source_target_pairs={{0,1},{1,2},{2,3},{3,4},{4,5},{5,6},{6,7},{7,8},{8,9},{9,10},{10,1... | collective-permute-start | bytes 6152 | tf_op jit(solution)/shard_map/ppermute | solution.py:118
  68.0 5.7 %collective-permute-start.10 = (bf16[2,512]{1,0:T(2,128)(2,1)S(1)}, bf16[2,512]{1,0:T(2,128)(2,1)S(1)}, u32[]{:S(2)}, u32[]{:S(2)}) collective-permute-start(bf16[2,512]{1,0:T(2,128)(2,1)S(1)} %collective-permute-done.9), channel_id=1, source_target_pairs={{0,1},{1,2},{2,3},{3,4},{4,5},{5,6},{6,7},{7,8},{8,9},{9,10},{10,1... | collective-permute-start | bytes 6152 | tf_op jit(solution)/shard_map/ppermute | solution.py:118
  73.7 5.7 %collective-permute-start.11 = (bf16[2,512]{1,0:T(2,128)(2,1)S(1)}, bf16[2,512]{1,0:T(2,128)(2,1)S(1)}, u32[]{:S(2)}, u32[]{:S(2)}) collective-permute-start(bf16[2,512]{1,0:T(2,128)(2,1)S(1)} %collective-permute-done.10), channel_id=1, source_target_pairs={{0,1},{1,2},{2,3},{3,4},{4,5},{5,6},{6,7},{7,8},{8,9},{9,10},{10,1... | collective-permute-start | bytes 6152 | tf_op jit(solution)/shard_map/ppermute | solution.py:118
  79.4 5.7 %collective-permute-start.12 = (bf16[2,512]{1,0:T(2,128)(2,1)S(1)}, bf16[2,512]{1,0:T(2,128)(2,1)S(1)}, u32[]{:S(2)}, u32[]{:S(2)}) collective-permute-start(bf16[2,512]{1,0:T(2,128)(2,1)S(1)} %collective-permute-done.11), channel_id=1, source_target_pairs={{0,1},{1,2},{2,3},{3,4},{4,5},{5,6},{6,7},{7,8},{8,9},{9,10},{10,1... | collective-permute-start | bytes 6152 | tf_op jit(solution)/shard_map/ppermute | solution.py:118
  85.1 5.7 %collective-permute-start.13 = (bf16[2,512]{1,0:T(2,128)(2,1)S(1)}, bf16[2,512]{1,0:T(2,128)(2,1)S(1)}, u32[]{:S(2)}, u32[]{:S(2)}) collective-permute-start(bf16[2,512]{1,0:T(2,128)(2,1)S(1)} %collective-permute-done.12), channel_id=1, source_target_pairs={{0,1},{1,2},{2,3},{3,4},{4,5},{5,6},{6,7},{7,8},{8,9},{9,10},{10,1... | collective-permute-start | bytes 6152 | tf_op jit(solution)/shard_map/ppermute | solution.py:118
  90.8 5.7 %collective-permute-start.14 = (bf16[2,512]{1,0:T(2,128)(2,1)S(1)}, bf16[2,512]{1,0:T(2,128)(2,1)S(1)}, u32[]{:S(2)}, u32[]{:S(2)}) collective-permute-start(bf16[2,512]{1,0:T(2,128)(2,1)S(1)} %collective-permute-done.13), channel_id=1, source_target_pairs={{0,1},{1,2},{2,3},{3,4},{4,5},{5,6},{6,7},{7,8},{8,9},{9,10},{10,1... | collective-permute-start | bytes 6152 | tf_op jit(solution)/shard_map/ppermute | solution.py:118
  98.6 1.0 copy-start.4
  98.6 1.3 copy-start.8
  105.0 61.2 %copy-start.5 = (bf16[2,2048]{1,0:T(2,128)(2,1)S(1)}, bf16[2,2048]{1,0:T(2,128)(2,1)}, u32[]{:S(2)}) copy-start(bf16[2,2048]{1,0:T(2,128)(2,1)} %param.8) | copy-start | bytes 24580
  306.8 5.4 %copy-start.3 = (f32[512,512]{1,0:T(8,128)S(1)}, f32[512,512]{1,0:T(8,128)}, u32[]{:S(2)}) copy-start(f32[512,512]{1,0:T(8,128)} %get-tuple-element.34) | copy-start | bytes 3145732
  312.3 1.6 copy-start.2
Sparse Core Ops, SparseCore 0:
  169.3 137.4 all-reduce.4
